TPU v7x, 512 devices: a whole 4x4x16 slice. The times are simulated.
512 devices in a mesh: gx: 32 (over z_hi, x, core), gy: 16 (over y, z_lo).
Axes of the slice: x: 4, y: 4, z: 16 (z_hi: 4, z_lo: 4; z = z_hi * 4 + z_lo), core: 2. Of those that a mesh axis runs over, the one named last changes fastest.
Arguments:
- orbitals: float32 [32, 64, 128, 512], P(None, 'gx', 'gy'), may hold values from -60 to 60
- potential: float32 [64, 128, 512], P('gx', 'gy'), may hold values from 0.2 to 2
- sign_bits: int32 [64, 128, 512], P('gx', 'gy'), may hold values from 0 to 1
- sampled_rows: int32 [32, 16, 8192], P('gx', 'gy'), may hold values from 0 to 8191, each once within a row
Outputs:
- rotated: float32 [32, 64, 128, 512], P(None, 'gx', 'gy')
- sketches: float32 [2, 32, 4096], P(None, None, ('gx', 'gy'))
- projected: float32 [32, 32], replicated
Inputs may be any that keep to these rules, and one draw needn't show every extreme that they name: Each block's row of sampled_rows holds every one of its 8192 cell numbers once.
All inputs are finite; a program needn't handle non-finite values.
Results may differ from a plain program's by a relative error of at most 0.00026.
Values sent between devices are 32-bit elements; how exact they have to be, the bound alone decides.
No kernel may reach another device: no remote copies, remote signals or barrier semaphores. Data moves between devices by JAX's collectives and lax.ppermute only.
A program may use at most 64 MiB of HBM per device.

v0:
```python
import jax
import jax.numpy as jnp
from jax import lax
from jax.sharding import PartitionSpec as P

M = 4096
HIGHEST = lax.Precision.HIGHEST
filter_center = 6.25
filter_half = 4.25


def padded_2(array, sides, width):
    for axis, dim in sides:
        size, length = (lax.axis_size(axis), array.shape[dim])
        up = [(i, (i + 1) % size) for i in range(size - 1)]
        down = [(j, i) for i, j in up]
        last = lax.slice_in_dim(array, length - width, length, axis=dim)
        initial = lax.slice_in_dim(array, 0, width, axis=dim)
        before = lax.ppermute(last, axis, up)
        after = lax.ppermute(initial, axis, down)
        array = jnp.concatenate([before, array, after], axis=dim)
    return array


def hadamard_table(order):
    index = jnp.arange(order, dtype=jnp.int32)
    parity = jnp.zeros((order, order), jnp.int32)
    for bit in range(order.bit_length() - 1):
        weight = 2**bit
        parity = parity + index[:, None] // weight % 2 * (index[None, :] // weight % 2)
    return (1 - 2 * (parity % 2)).astype(jnp.float32)


def second_diff(padded, axis, count):
    parts = [lax.slice_in_dim(padded, k, k + count, axis=axis) for k in range(5)]
    return (16.0 * (parts[1] + parts[3]) - (parts[0] + parts[4]) - 30.0 * parts[2]) / 12.0


def apply_ham(field, potential):
    padded = padded_2(field, (("gx", 1), ("gy", 2)), 2)
    x_padded = padded[:, :, 2:-2, :]
    y_padded = padded[:, 2:-2, :, :]
    z_padded = jnp.pad(field, ((0, 0), (0, 0), (0, 0), (2, 2)))
    total = second_diff(x_padded, 1, field.shape[1])
    total = total + second_diff(y_padded, 2, field.shape[2])
    total = total + second_diff(z_padded, 3, field.shape[3])
    return -0.5 * total + potential[None] * field


def shards(orbitals, potential, sign_bits, sampled_rows):
    first = (apply_ham(orbitals, potential) - filter_center * orbitals) / filter_half
    second = 2.0 * (apply_ham(first, potential) - filter_center * first) / filter_half - orbitals
    filtered = 2.0 * (apply_ham(second, potential) - filter_center * second) / filter_half - first
    applied = apply_ham(filtered, potential)
    count = orbitals.shape[0]
    cells = orbitals.shape[1] * orbitals.shape[2] * orbitals.shape[3]
    stacked = jnp.concatenate([filtered, applied], axis=0)
    sign_block = (2 * sign_bits - 1).astype(jnp.float32)
    flat = (stacked * sign_block[None]).reshape(2 * count, -1, 128)
    mixed = jnp.einsum("nac,cd->nad", flat, hadamard_table(128), precision=HIGHEST)
    mixed = jnp.einsum("ba,nac->nbc", hadamard_table(cells // 128), mixed, precision=HIGHEST)
    mixed = mixed.reshape(2 * count, cells)
    picked = jnp.take(mixed, sampled_rows[0, 0, :M], axis=1)
    devices = lax.axis_size("gx") * lax.axis_size("gy")
    term = (picked / jnp.sqrt(jnp.float32(M * devices))).reshape(2, count, M)
    width = M // devices
    total = lax.psum(term, ("gx", "gy"))
    position = lax.axis_index("gx") * lax.axis_size("gy") + lax.axis_index("gy")
    share = lax.dynamic_slice_in_dim(total, position * width, width, 2)
    gram = jnp.dot(total[0], total[0].T, precision=HIGHEST) / cells
    cross = jnp.dot(total[0], total[1].T, precision=HIGHEST) / cells
    lower = jnp.linalg.cholesky(gram)
    inverse = lax.linalg.triangular_solve(
        lower, jnp.eye(count, dtype=jnp.float32), left_side=True, lower=True
    )
    rotated = jnp.dot(inverse, filtered.reshape(count, -1), precision=HIGHEST).reshape(
        filtered.shape
    )
    inner = jnp.dot(jnp.dot(inverse, cross, precision=HIGHEST), inverse.T, precision=HIGHEST)
    projected = 0.5 * (inner + inner.T)
    return (rotated, share, projected)


def solution(mesh):
    in_specs = (
        P(None, "gx", "gy", None),
        P("gx", "gy", None),
        P("gx", "gy", None),
        P("gx", "gy", None),
    )
    out_specs = (P(None, "gx", "gy", None), P(None, None, ("gx", "gy")), P())
    return jax.shard_map(shards, mesh=mesh, in_specs=in_specs, out_specs=out_specs, check_vma=False)
```

profile of v0, /device:TPU:1, one launch (start us, length us, event | category | flops | bytes accessed | tf_op | source)
XLA Modules:
  0.0 938.2 jit_solution(11268816920238034277)
XLA Ops:
  9.1 4.5 collective-permute-start
  13.7 5.6 collective-permute-start.1
  19.3 6.1 collective-permute-done
  26.1 4.0 collective-permute-done.1
  30.3 3.6 collective-permute-start.2
  35.2 7.6 collective-permute-done.2
  42.8 28.2 %collective-permute-done.3 = f32[32,6,2,512]{3,0,2,1:T(8,128)S(1)} collective-permute-done((f32[32,6,2,512]{3,0,2,1:T(8,128)S(1)}, f32[32,6,2,512]{3,0,2,1:T(8,128)S(1)}, u32[]{:S(2)}, u32[]{:S(2)}) %collective-permute-start.3) | collective-permute-done | bytes 786464 | tf_op jit(solution)/shard_map/ppermute | solution.py:20
  72.6 2.7 collective-permute-start.4
  77.3 9.8 %collective-permute-done.4 = f32[32,2,8,512]{3,0,2,1:T(8,128)S(1)} collective-permute-done((f32[32,2,8,512]{3,0,2,1:T(8,128)S(1)}, f32[32,2,8,512]{3,0,2,1:T(8,128)S(1)}, u32[]{:S(2)}, u32[]{:S(2)}) %collective-permute-start.4) | collective-permute-done | bytes 1048608 | tf_op jit(solution)/shard_map/ppermute | solution.py:19
  87.1 4.4 collective-permute-done.5
  91.6 7.8 collective-permute-start.6
  100.7 7.6 collective-permute-done.6
  108.2 26.3 %collective-permute-done.7 = f32[32,6,2,512]{3,0,2,1:T(8,128)S(1)} collective-permute-done((f32[32,6,2,512]{3,0,2,1:T(8,128)S(1)}, f32[32,6,2,512]{3,0,2,1:T(8,128)S(1)}, u32[]{:S(2)}, u32[]{:S(2)}) %collective-permute-start.7) | collective-permute-done | bytes 786464 | tf_op jit(solution)/shard_map/ppermute | solution.py:20
  134.6 2.4 fusion.21
  138.9 2.5 collective-permute-start.9
  141.3 9.2 collective-permute-done.8
  150.6 4.4 collective-permute-done.9
  155.1 3.0 collective-permute-start.10
  159.5 7.5 collective-permute-done.10
  167.0 24.4 %collective-permute-done.11 = f32[32,6,2,512]{3,0,2,1:T(8,128)S(1)} collective-permute-done((f32[32,6,2,512]{3,0,2,1:T(8,128)S(1)}, f32[32,6,2,512]{3,0,2,1:T(8,128)S(1)}, u32[]{:S(2)}, u32[]{:S(2)}) %collective-permute-start.11) | collective-permute-done | bytes 786464 | tf_op jit(solution)/shard_map/ppermute | solution.py:20
  195.1 2.5 collective-permute-start.13
  197.7 9.1 collective-permute-done.12
  206.8 22.0 %collective-permute-done.13 = f32[32,2,8,512]{3,0,2,1:T(8,128)S(1)} collective-permute-done((f32[32,2,8,512]{3,0,2,1:T(8,128)S(1)}, f32[32,2,8,512]{3,0,2,1:T(8,128)S(1)}, u32[]{:S(2)}, u32[]{:S(2)}) %collective-permute-start.13) | collective-permute-done | bytes 1048608 | tf_op jit(solution)/shard_map/ppermute | solution.py:20
  230.3 3.5 collective-permute-start.14
  235.7 6.3 collective-permute-done.14
  242.1 27.8 %collective-permute-done.15 = f32[32,6,2,512]{3,0,2,1:T(8,128)} collective-permute-done((f32[32,6,2,512]{3,0,2,1:T(8,128)}, f32[32,6,2,512]{3,0,2,1:T(8,128)}, u32[]{:S(2)}, u32[]{:S(2)}) %collective-permute-start.15) | collective-permute-done | bytes 786464 | tf_op jit(solution)/shard_map/ppermute | solution.py:20
  269.9 3.4 fusion.40
  280.2 2.7 copy.57
  282.9 13.0 %gather_fusion = f32[4096,64]{1,0:T(8,128)S(1)} fusion(f32[64,8192]{0,1:T(8,128)} %bitcast.60, s32[4096]{0:T(1024)S(1)} %broadcast_clamp_fusion), kind=kCustom, calls=%fused_computation | custom fusion | bytes 2113536 | tf_op jit(solution)/shard_map/jit(_take)/gather | solution.py:63
  300.4 614.8 %all-reduce.6.cloned.1.call-done = f32[2,32,4096]{2,1,0:T(8,128)} async-done(((f32[2,32,4096]{2,1,0:T(8,128)}), f32[2,32,4096]{2,1,0:T(8,128)}) %all-reduce.6.cloned.1.call-update) | async-done | bytes 1048592 | tf_op jit(solution)/shard_map/psum | solution.py:67
  917.0 2.9 cholesky.17
  921.3 2.4 custom-call.6
  (71 shorter events, 41.9 us)
Async XLA Ops:
  7.2 18.3 %copy-start = (f32[32,2,8,512]{3,2,1,0:T(8,128)S(1)}, f32[32,2,8,512]{3,2,1,0:T(8,128)}, u32[]{:S(2)}) copy-start(f32[32,2,8,512]{3,2,1,0:T(8,128)} %param.4) | copy-start | bytes 3145732
  7.2 908.0 %all-reduce.6.cloned.1.call-start = ((), (), s32[]{:S(2)}) async-start(), calls=%async_computation | async-start | bytes 2097152 | tf_op jit(solution)/shard_map/psum | solution.py:67
  9.1 16.2 %collective-permute-start = (f32[32,2,8,512]{3,0,2,1:T(8,128)S(1)}, f32[32,2,8,512]{3,0,2,1:T(8,128)S(1)}, u32[]{:S(2)}, u32[]{:S(2)}) collective-permute-start(f32[32,2,8,512]{3,0,2,1:T(8,128)S(1)} %copy.36), channel_id=1, source_target_pairs={{0,16},{16,32},{32,48},{48,64},{64,80},{80,96},{96,112},{112,128},... | collective-permute-start | bytes 3145736 | tf_op jit(solution)/shard_map/ppermute | solution.py:19
  13.7 16.4 %collective-permute-start.1 = (f32[32,2,8,512]{3,0,2,1:T(8,128)S(1)}, f32[32,2,8,512]{3,0,2,1:T(8,128)S(1)}, u32[]{:S(2)}, u32[]{:S(2)}) collective-permute-start(f32[32,2,8,512]{3,0,2,1:T(8,128)S(1)} %copy.36), channel_id=1, source_target_pairs={{16,0},{32,16},{48,32},{64,48},{80,64},{96,80},{112,96},{128,112},... | collective-permute-start | bytes 3145736 | tf_op jit(solution)/shard_map/ppermute | solution.py:20
  30.2 40.8 %copy-start.3 = (f32[2,8,512]{2,1,0:T(8,128)S(1)}, f32[2,8,512]{2,1,0:T(8,128)}, u32[]{:S(2)}) copy-start(f32[2,8,512]{2,1,0:T(8,128)} %param.5) | copy-start | bytes 98308
  30.3 12.5 %collective-permute-start.2 = (f32[32,6,2,512]{3,0,2,1:T(8,128)S(1)}, f32[32,6,2,512]{3,0,2,1:T(8,128)S(1)}, u32[]{:S(2)}, u32[]{:S(2)}) collective-permute-start(f32[32,6,2,512]{3,0,2,1:T(8,128)S(1)} %get-tuple-element.23), channel_id=1, source_target_pairs={{0,1},{1,2},{2,3},{3,4},{4,5},{5,6},{6,7},{7,8},{8,9},{9,10},{10,1... | collective-permute-start | bytes 2359304 | tf_op jit(solution)/shard_map/ppermute | solution.py:19
  33.9 37.1 %collective-permute-start.3 = (f32[32,6,2,512]{3,0,2,1:T(8,128)S(1)}, f32[32,6,2,512]{3,0,2,1:T(8,128)S(1)}, u32[]{:S(2)}, u32[]{:S(2)}) collective-permute-start(f32[32,6,2,512]{3,0,2,1:T(8,128)S(1)} %get-tuple-element.24), channel_id=1, source_target_pairs={{1,0},{2,1},{3,2},{4,3},{5,4},{6,5},{7,6},{8,7},{9,8},{10,9},{11,1... | collective-permute-start | bytes 2359304 | tf_op jit(solution)/shard_map/ppermute | solution.py:20
  72.6 14.4 %collective-permute-start.4 = (f32[32,2,8,512]{3,0,2,1:T(8,128)S(1)}, f32[32,2,8,512]{3,0,2,1:T(8,128)S(1)}, u32[]{:S(2)}, u32[]{:S(2)}) collective-permute-start(f32[32,2,8,512]{3,0,2,1:T(8,128)S(1)} %get-tuple-element.15), channel_id=1, source_target_pairs={{0,16},{16,32},{32,48},{48,64},{64,80},{80,96},{96,112},{112,128},... | collective-permute-start | bytes 3145736 | tf_op jit(solution)/shard_map/ppermute | solution.py:19
  75.3 16.1 %collective-permute-start.5 = (f32[32,2,8,512]{3,0,2,1:T(8,128)S(1)}, f32[32,2,8,512]{3,0,2,1:T(8,128)S(1)}, u32[]{:S(2)}, u32[]{:S(2)}) collective-permute-start(f32[32,2,8,512]{3,0,2,1:T(8,128)S(1)} %get-tuple-element.15), channel_id=1, source_target_pairs={{16,0},{32,16},{48,32},{64,48},{80,64},{96,80},{112,96},{128,112},... | collective-permute-start | bytes 3145736 | tf_op jit(solution)/shard_map/ppermute | solution.py:20
  91.6 16.7 %collective-permute-start.6 = (f32[32,6,2,512]{3,0,2,1:T(8,128)S(1)}, f32[32,6,2,512]{3,0,2,1:T(8,128)S(1)}, u32[]{:S(2)}, u32[]{:S(2)}) collective-permute-start(f32[32,6,2,512]{3,0,2,1:T(8,128)S(1)} %get-tuple-element.21), channel_id=1, source_target_pairs={{0,1},{1,2},{2,3},{3,4},{4,5},{5,6},{6,7},{7,8},{8,9},{9,10},{10,1... | collective-permute-start | bytes 2359304 | tf_op jit(solution)/shard_map/ppermute | solution.py:19
  99.4 35.2 %collective-permute-start.7 = (f32[32,6,2,512]{3,0,2,1:T(8,128)S(1)}, f32[32,6,2,512]{3,0,2,1:T(8,128)S(1)}, u32[]{:S(2)}, u32[]{:S(2)}) collective-permute-start(f32[32,6,2,512]{3,0,2,1:T(8,128)S(1)} %get-tuple-element.22), channel_id=1, source_target_pairs={{1,0},{2,1},{3,2},{4,3},{5,4},{6,5},{7,6},{8,7},{9,8},{10,9},{11,1... | collective-permute-start | bytes 2359304 | tf_op jit(solution)/shard_map/ppermute | solution.py:20
  136.9 13.7 %collective-permute-start.8 = (f32[32,2,8,512]{3,0,2,1:T(8,128)S(1)}, f32[32,2,8,512]{3,0,2,1:T(8,128)S(1)}, u32[]{:S(2)}, u32[]{:S(2)}) collective-permute-start(f32[32,2,8,512]{3,0,2,1:T(8,128)S(1)} %fusion.21), channel_id=1, source_target_pairs={{0,16},{16,32},{32,48},{48,64},{64,80},{80,96},{96,112},{112,128},... | collective-permute-start | bytes 3145736 | tf_op jit(solution)/shard_map/ppermute | solution.py:19
  138.9 16.1 %collective-permute-start.9 = (f32[32,2,8,512]{3,0,2,1:T(8,128)S(1)}, f32[32,2,8,512]{3,0,2,1:T(8,128)S(1)}, u32[]{:S(2)}, u32[]{:S(2)}) collective-permute-start(f32[32,2,8,512]{3,0,2,1:T(8,128)S(1)} %fusion.21), channel_id=1, source_target_pairs={{16,0},{32,16},{48,32},{64,48},{80,64},{96,80},{112,96},{128,112},... | collective-permute-start | bytes 3145736 | tf_op jit(solution)/shard_map/ppermute | solution.py:20
  155.1 11.9 %collective-permute-start.10 = (f32[32,6,2,512]{3,0,2,1:T(8,128)S(1)}, f32[32,6,2,512]{3,0,2,1:T(8,128)S(1)}, u32[]{:S(2)}, u32[]{:S(2)}) collective-permute-start(f32[32,6,2,512]{3,0,2,1:T(8,128)S(1)} %get-tuple-element.19), channel_id=1, source_target_pairs={{0,1},{1,2},{2,3},{3,4},{4,5},{5,6},{6,7},{7,8},{8,9},{9,10},{10,1... | collective-permute-start | bytes 2359304 | tf_op jit(solution)/shard_map/ppermute | solution.py:19
  158.1 39.4 %copy-start.5 = (s32[2,8,512]{2,1,0:T(8,128)S(1)}, s32[2,8,512]{2,1,0:T(8,128)}, u32[]{:S(2)}) copy-start(s32[2,8,512]{2,1,0:T(8,128)} %param.6) | copy-start | bytes 98308
  158.2 39.5 %slice-start = ((s32[1,1,8192]{2,1,0:T(1,128)}), s32[1,1,4096]{2,1,0:T(1,128)S(1)}, s32[]{:S(2)}) async-start(s32[1,1,8192]{2,1,0:T(1,128)} %param.7), calls=%async_computation.1 | async-start | bytes 32768 | tf_op jit(solution)/shard_map/slice | solution.py:63
  158.2 33.2 %collective-permute-start.11 = (f32[32,6,2,512]{3,0,2,1:T(8,128)S(1)}, f32[32,6,2,512]{3,0,2,1:T(8,128)S(1)}, u32[]{:S(2)}, u32[]{:S(2)}) collective-permute-start(f32[32,6,2,512]{3,0,2,1:T(8,128)S(1)} %get-tuple-element.20), channel_id=1, source_target_pairs={{1,0},{2,1},{3,2},{4,3},{5,4},{6,5},{7,6},{8,7},{9,8},{10,9},{11,1... | collective-permute-start | bytes 2359304 | tf_op jit(solution)/shard_map/ppermute | solution.py:20
  193.2 13.7 %collective-permute-start.12 = (f32[32,2,8,512]{3,0,2,1:T(8,128)S(1)}, f32[32,2,8,512]{3,0,2,1:T(8,128)S(1)}, u32[]{:S(2)}, u32[]{:S(2)}) collective-permute-start(f32[32,2,8,512]{3,0,2,1:T(8,128)S(1)} %fusion.32), channel_id=1, source_target_pairs={{0,16},{16,32},{32,48},{48,64},{64,80},{80,96},{96,112},{112,128},... | collective-permute-start | bytes 3145736 | tf_op jit(solution)/shard_map/ppermute | solution.py:19
  195.1 33.7 %collective-permute-start.13 = (f32[32,2,8,512]{3,0,2,1:T(8,128)S(1)}, f32[32,2,8,512]{3,0,2,1:T(8,128)S(1)}, u32[]{:S(2)}, u32[]{:S(2)}) collective-permute-start(f32[32,2,8,512]{3,0,2,1:T(8,128)S(1)} %fusion.32), channel_id=1, source_target_pairs={{16,0},{32,16},{48,32},{64,48},{80,64},{96,80},{112,96},{128,112},... | collective-permute-start | bytes 3145736 | tf_op jit(solution)/shard_map/ppermute | solution.py:20
  197.7 37.3 %copy-start.4 = (s32[1,1,8192]{2,1,0:T(1,128)S(1)}, s32[1,1,8192]{2,1,0:T(1,128)}, u32[]{:S(2)}) copy-start(s32[1,1,8192]{2,1,0:T(1,128)} %param.7) | copy-start | bytes 98308
  206.8 23.4 %copy-start.1 = (f32[32,2,8,512]{3,0,2,1:T(8,128)}, f32[32,2,8,512]{3,0,2,1:T(8,128)S(1)}, u32[]{:S(2)}) copy-start(f32[32,2,8,512]{3,0,2,1:T(8,128)S(1)} %collective-permute-done.12) | copy-start | bytes 3145732
  228.8 1.5 copy-start.2
  230.3 11.8 %collective-permute-start.14 = (f32[32,6,2,512]{3,0,2,1:T(8,128)}, f32[32,6,2,512]{3,0,2,1:T(8,128)}, u32[]{:S(2)}, u32[]{:S(2)}) collective-permute-start(f32[32,6,2,512]{3,0,2,1:T(8,128)} %get-tuple-element.17), channel_id=1, source_target_pairs={{0,1},{1,2},{2,3},{3,4},{4,5},{5,6},{6,7},{7,8},{8,9},{9,10},{10,1... | collective-permute-start | bytes 2359304 | tf_op jit(solution)/shard_map/ppermute | solution.py:19
  233.7 36.1 %collective-permute-start.15 = (f32[32,6,2,512]{3,0,2,1:T(8,128)}, f32[32,6,2,512]{3,0,2,1:T(8,128)}, u32[]{:S(2)}, u32[]{:S(2)}) collective-permute-start(f32[32,6,2,512]{3,0,2,1:T(8,128)} %get-tuple-element.18), channel_id=1, source_target_pairs={{1,0},{2,1},{3,2},{4,3},{5,4},{6,5},{7,6},{8,7},{9,8},{10,9},{11,1... | collective-permute-start | bytes 2359304 | tf_op jit(solution)/shard_map/ppermute | solution.py:20
Sparse Core Ops, SparseCore 0:
  299.9 615.2 all-reduce.5
where the time goes:
time: 939 us; the launch traced here: 938 us
  waiting for transfers between devices  819 us (87%)
  starting transfers between devices  46.6 us (5%)
  local copies, waits for them, and re-layouts  27.6 us (3%)
  other arithmetic  20.5 us (2%)
  between operations  14.5 us (2%)
  matrix products  9.67 us (1%)
    psum x1, waiting for transfers between devices, shards(): total = lax.psum(term, ('gx', 'gy'))  615 us
    ppermute x8, waiting for transfers between devices, padded_2(): after = lax.ppermute(initial, axis, down)  141 us
    ppermute x8, waiting for transfers between devices, padded_2(): before = lax.ppermute(last, axis, up)  63.2 us
    ppermute x8, starting transfers between devices, padded_2(): before = lax.ppermute(last, axis, up)  28.9 us
  transfers between devices with their start and end apart: 17, of which 17 were waited for; matrix products, arithmetic and copies ran while one was open for 0% of the time, Pallas kernels for 0%

commit v1 on v0

--- a/solution.py
+++ b/solution.py
@@ -64,7 +64,9 @@
     devices = lax.axis_size("gx") * lax.axis_size("gy")
     term = (picked / jnp.sqrt(jnp.float32(M * devices))).reshape(2, count, M)
     width = M // devices
-    total = lax.psum(term, ("gx", "gy"))
+    total = term
+    for ii in ("gx", "gy"):
+        total = lax.psum(total, ii)
     position = lax.axis_index("gx") * lax.axis_size("gy") + lax.axis_index("gy")
     share = lax.dynamic_slice_in_dim(total, position * width, width, 2)
     gram = jnp.dot(total[0], total[0].T, precision=HIGHEST) / cells

time: 939 us -> 1000 us (1.065)
  waiting for transfers between devices: 819 us -> 872 us
    psum x1 -> x2, waiting for transfers between devices: 615 us -> 668 us  [shards(): total = lax.psum(total, ii)]
  transfers between devices with their start and end apart: 17 -> 18, of which waited for: 17 -> 18; matrix products, arithmetic and copies ran while one was open for 0% -> 0% of each run, Pallas kernels for 0% -> 0%
where the time goes in v1:
time: 1000 us; the launch traced here: 991 us
  waiting for transfers between devices  872 us (87%)
  starting transfers between devices  47 us (5%)
  local copies, waits for them, and re-layouts  27.6 us (3%)
  other arithmetic  20.3 us (2%)
  between operations  14.5 us (1%)
    psum x2, waiting for transfers between devices, shards(): total = lax.psum(total, ii)  668 us
    ppermute x8, waiting for transfers between devices, padded_2(): after = lax.ppermute(initial, axis, down)  141 us
    ppermute x8, waiting for transfers between devices, padded_2(): before = lax.ppermute(last, axis, up)  63 us
    ppermute x8, starting transfers between devices, padded_2(): before = lax.ppermute(last, axis, up)  28.9 us
  transfers between devices with their start and end apart: 18, of which 18 were waited for; matrix products, arithmetic and copies ran while one was open for 0% of the time, Pallas kernels for 0%

profile of v1, /device:TPU:1, one launch (start us, length us, event | category | flops | bytes accessed | tf_op | source)
XLA Modules:
  0.0 991.1 jit_solution(15350385359573245340)
XLA Ops:
  9.1 4.5 collective-permute-start
  13.7 5.6 collective-permute-start.1
  19.3 6.1 collective-permute-done
  26.1 4.0 collective-permute-done.1
  30.3 3.6 collective-permute-start.2
  35.2 7.6 collective-permute-done.2
  42.8 28.2 %collective-permute-done.3 = f32[32,6,2,512]{3,0,2,1:T(8,128)S(1)} collective-permute-done((f32[32,6,2,512]{3,0,2,1:T(8,128)S(1)}, f32[32,6,2,512]{3,0,2,1:T(8,128)S(1)}, u32[]{:S(2)}, u32[]{:S(2)}) %collective-permute-start.3) | collective-permute-done | bytes 786464 | tf_op jit(solution)/shard_map/ppermute | solution.py:20
  72.6 2.7 collective-permute-start.4
  77.3 9.8 collective-permute-done.4
  87.1 4.4 collective-permute-done.5
  91.6 7.8 collective-permute-start.6
  100.7 7.6 collective-permute-done.6
  108.2 26.3 %collective-permute-done.7 = f32[32,6,2,512]{3,0,2,1:T(8,128)S(1)} collective-permute-done((f32[32,6,2,512]{3,0,2,1:T(8,128)S(1)}, f32[32,6,2,512]{3,0,2,1:T(8,128)S(1)}, u32[]{:S(2)}, u32[]{:S(2)}) %collective-permute-start.7) | collective-permute-done | bytes 786464 | tf_op jit(solution)/shard_map/ppermute | solution.py:20
  138.9 2.5 collective-permute-start.9
  141.3 9.2 collective-permute-done.8
  150.6 4.4 collective-permute-done.9
  155.1 3.0 collective-permute-start.10
  159.5 7.5 collective-permute-done.10
  167.0 24.4 %collective-permute-done.11 = f32[32,6,2,512]{3,0,2,1:T(8,128)S(1)} collective-permute-done((f32[32,6,2,512]{3,0,2,1:T(8,128)S(1)}, f32[32,6,2,512]{3,0,2,1:T(8,128)S(1)}, u32[]{:S(2)}, u32[]{:S(2)}) %collective-permute-start.11) | collective-permute-done | bytes 786464 | tf_op jit(solution)/shard_map/ppermute | solution.py:20
  195.1 2.5 collective-permute-start.13
  197.7 9.1 collective-permute-done.12
  206.8 22.0 %collective-permute-done.13 = f32[32,2,8,512]{3,0,2,1:T(8,128)S(1)} collective-permute-done((f32[32,2,8,512]{3,0,2,1:T(8,128)S(1)}, f32[32,2,8,512]{3,0,2,1:T(8,128)S(1)}, u32[]{:S(2)}, u32[]{:S(2)}) %collective-permute-start.13) | collective-permute-done | bytes 1048608 | tf_op jit(solution)/shard_map/ppermute | solution.py:20
  230.3 3.5 collective-permute-start.14
  235.9 6.1 collective-permute-done.14
  242.1 27.8 %collective-permute-done.15 = f32[32,6,2,512]{3,0,2,1:T(8,128)} collective-permute-done((f32[32,6,2,512]{3,0,2,1:T(8,128)}, f32[32,6,2,512]{3,0,2,1:T(8,128)}, u32[]{:S(2)}, u32[]{:S(2)}) %collective-permute-start.15) | collective-permute-done | bytes 786464 | tf_op jit(solution)/shard_map/ppermute | solution.py:20
  269.9 3.2 fusion.40
  280.0 2.7 copy.57
  282.8 13.0 %gather_fusion = f32[4096,64]{1,0:T(8,128)S(1)} fusion(f32[64,8192]{0,1:T(8,128)} %bitcast.60, s32[4096]{0:T(1024)S(1)} %broadcast_clamp_fusion), kind=kCustom, calls=%fused_computation | custom fusion | bytes 2113536 | tf_op jit(solution)/shard_map/jit(_take)/gather | solution.py:63
  299.9 499.0 %all-reduce.7.cloned.1.call-done = f32[2,32,4096]{2,1,0:T(8,128)} async-done(((f32[2,32,4096]{2,1,0:T(8,128)}), f32[2,32,4096]{2,1,0:T(8,128)}) %all-reduce.7.cloned.1.call-update) | async-done | bytes 1048592 | tf_op jit(solution)/shard_map/psum | solution.py:69
  799.6 168.5 %all-reduce.9.cloned.1.call-done = f32[2,32,4096]{2,1,0:T(8,128)} async-done(((f32[2,32,4096]{2,1,0:T(8,128)}), f32[2,32,4096]{2,1,0:T(8,128)}) %all-reduce.9.cloned.1.call-update) | async-done | bytes 1048592 | tf_op jit(solution)/shard_map/psum | solution.py:69
  969.9 2.9 cholesky.17
  974.1 2.4 custom-call.6
  (74 shorter events, 44.8 us)
Async XLA Ops:
  7.2 18.3 %copy-start = (f32[32,2,8,512]{3,2,1,0:T(8,128)S(1)}, f32[32,2,8,512]{3,2,1,0:T(8,128)}, u32[]{:S(2)}) copy-start(f32[32,2,8,512]{3,2,1,0:T(8,128)} %param.4) | copy-start | bytes 3145732
  7.2 791.8 %all-reduce.7.cloned.1.call-start = ((), (), s32[]{:S(2)}) async-start(), calls=%async_computation | async-start | bytes 2097152 | tf_op jit(solution)/shard_map/psum | solution.py:69
  9.1 16.2 %collective-permute-start = (f32[32,2,8,512]{3,0,2,1:T(8,128)S(1)}, f32[32,2,8,512]{3,0,2,1:T(8,128)S(1)}, u32[]{:S(2)}, u32[]{:S(2)}) collective-permute-start(f32[32,2,8,512]{3,0,2,1:T(8,128)S(1)} %copy.36), channel_id=1, source_target_pairs={{0,16},{16,32},{32,48},{48,64},{64,80},{80,96},{96,112},{112,128},... | collective-permute-start | bytes 3145736 | tf_op jit(solution)/shard_map/ppermute | solution.py:19
  13.7 16.4 %collective-permute-start.1 = (f32[32,2,8,512]{3,0,2,1:T(8,128)S(1)}, f32[32,2,8,512]{3,0,2,1:T(8,128)S(1)}, u32[]{:S(2)}, u32[]{:S(2)}) collective-permute-start(f32[32,2,8,512]{3,0,2,1:T(8,128)S(1)} %copy.36), channel_id=1, source_target_pairs={{16,0},{32,16},{48,32},{64,48},{80,64},{96,80},{112,96},{128,112},... | collective-permute-start | bytes 3145736 | tf_op jit(solution)/shard_map/ppermute | solution.py:20
  30.2 40.8 %copy-start.3 = (f32[2,8,512]{2,1,0:T(8,128)S(1)}, f32[2,8,512]{2,1,0:T(8,128)}, u32[]{:S(2)}) copy-start(f32[2,8,512]{2,1,0:T(8,128)} %param.5) | copy-start | bytes 98308
  30.3 12.5 %collective-permute-start.2 = (f32[32,6,2,512]{3,0,2,1:T(8,128)S(1)}, f32[32,6,2,512]{3,0,2,1:T(8,128)S(1)}, u32[]{:S(2)}, u32[]{:S(2)}) collective-permute-start(f32[32,6,2,512]{3,0,2,1:T(8,128)S(1)} %get-tuple-element.23), channel_id=1, source_target_pairs={{0,1},{1,2},{2,3},{3,4},{4,5},{5,6},{6,7},{7,8},{8,9},{9,10},{10,1... | collective-permute-start | bytes 2359304 | tf_op jit(solution)/shard_map/ppermute | solution.py:19
  33.9 37.1 %collective-permute-start.3 = (f32[32,6,2,512]{3,0,2,1:T(8,128)S(1)}, f32[32,6,2,512]{3,0,2,1:T(8,128)S(1)}, u32[]{:S(2)}, u32[]{:S(2)}) collective-permute-start(f32[32,6,2,512]{3,0,2,1:T(8,128)S(1)} %get-tuple-element.24), channel_id=1, source_target_pairs={{1,0},{2,1},{3,2},{4,3},{5,4},{6,5},{7,6},{8,7},{9,8},{10,9},{11,1... | collective-permute-start | bytes 2359304 | tf_op jit(solution)/shard_map/ppermute | solution.py:20
  72.6 14.4 %collective-permute-start.4 = (f32[32,2,8,512]{3,0,2,1:T(8,128)S(1)}, f32[32,2,8,512]{3,0,2,1:T(8,128)S(1)}, u32[]{:S(2)}, u32[]{:S(2)}) collective-permute-start(f32[32,2,8,512]{3,0,2,1:T(8,128)S(1)} %get-tuple-element.15), channel_id=1, source_target_pairs={{0,16},{16,32},{32,48},{48,64},{64,80},{80,96},{96,112},{112,128},... | collective-permute-start | bytes 3145736 | tf_op jit(solution)/shard_map/ppermute | solution.py:19
  75.3 16.1 %collective-permute-start.5 = (f32[32,2,8,512]{3,0,2,1:T(8,128)S(1)}, f32[32,2,8,512]{3,0,2,1:T(8,128)S(1)}, u32[]{:S(2)}, u32[]{:S(2)}) collective-permute-start(f32[32,2,8,512]{3,0,2,1:T(8,128)S(1)} %get-tuple-element.15), channel_id=1, source_target_pairs={{16,0},{32,16},{48,32},{64,48},{80,64},{96,80},{112,96},{128,112},... | collective-permute-start | bytes 3145736 | tf_op jit(solution)/shard_map/ppermute | solution.py:20
  91.6 16.7 %collective-permute-start.6 = (f32[32,6,2,512]{3,0,2,1:T(8,128)S(1)}, f32[32,6,2,512]{3,0,2,1:T(8,128)S(1)}, u32[]{:S(2)}, u32[]{:S(2)}) collective-permute-start(f32[32,6,2,512]{3,0,2,1:T(8,128)S(1)} %get-tuple-element.21), channel_id=1, source_target_pairs={{0,1},{1,2},{2,3},{3,4},{4,5},{5,6},{6,7},{7,8},{8,9},{9,10},{10,1... | collective-permute-start | bytes 2359304 | tf_op jit(solution)/shard_map/ppermute | solution.py:19
  99.4 35.2 %collective-permute-start.7 = (f32[32,6,2,512]{3,0,2,1:T(8,128)S(1)}, f32[32,6,2,512]{3,0,2,1:T(8,128)S(1)}, u32[]{:S(2)}, u32[]{:S(2)}) collective-permute-start(f32[32,6,2,512]{3,0,2,1:T(8,128)S(1)} %get-tuple-element.22), channel_id=1, source_target_pairs={{1,0},{2,1},{3,2},{4,3},{5,4},{6,5},{7,6},{8,7},{9,8},{10,9},{11,1... | collective-permute-start | bytes 2359304 | tf_op jit(solution)/shard_map/ppermute | solution.py:20
  136.9 13.7 %collective-permute-start.8 = (f32[32,2,8,512]{3,0,2,1:T(8,128)S(1)}, f32[32,2,8,512]{3,0,2,1:T(8,128)S(1)}, u32[]{:S(2)}, u32[]{:S(2)}) collective-permute-start(f32[32,2,8,512]{3,0,2,1:T(8,128)S(1)} %fusion.21), channel_id=1, source_target_pairs={{0,16},{16,32},{32,48},{48,64},{64,80},{80,96},{96,112},{112,128},... | collective-permute-start | bytes 3145736 | tf_op jit(solution)/shard_map/ppermute | solution.py:19
  138.9 16.1 %collective-permute-start.9 = (f32[32,2,8,512]{3,0,2,1:T(8,128)S(1)}, f32[32,2,8,512]{3,0,2,1:T(8,128)S(1)}, u32[]{:S(2)}, u32[]{:S(2)}) collective-permute-start(f32[32,2,8,512]{3,0,2,1:T(8,128)S(1)} %fusion.21), channel_id=1, source_target_pairs={{16,0},{32,16},{48,32},{64,48},{80,64},{96,80},{112,96},{128,112},... | collective-permute-start | bytes 3145736 | tf_op jit(solution)/shard_map/ppermute | solution.py:20
  155.1 11.9 %collective-permute-start.10 = (f32[32,6,2,512]{3,0,2,1:T(8,128)S(1)}, f32[32,6,2,512]{3,0,2,1:T(8,128)S(1)}, u32[]{:S(2)}, u32[]{:S(2)}) collective-permute-start(f32[32,6,2,512]{3,0,2,1:T(8,128)S(1)} %get-tuple-element.19), channel_id=1, source_target_pairs={{0,1},{1,2},{2,3},{3,4},{4,5},{5,6},{6,7},{7,8},{8,9},{9,10},{10,1... | collective-permute-start | bytes 2359304 | tf_op jit(solution)/shard_map/ppermute | solution.py:19
  158.1 39.4 %copy-start.5 = (s32[2,8,512]{2,1,0:T(8,128)S(1)}, s32[2,8,512]{2,1,0:T(8,128)}, u32[]{:S(2)}) copy-start(s32[2,8,512]{2,1,0:T(8,128)} %param.6) | copy-start | bytes 98308
  158.2 39.5 %slice-start = ((s32[1,1,8192]{2,1,0:T(1,128)}), s32[1,1,4096]{2,1,0:T(1,128)S(1)}, s32[]{:S(2)}) async-start(s32[1,1,8192]{2,1,0:T(1,128)} %param.7), calls=%async_computation.2 | async-start | bytes 32768 | tf_op jit(solution)/shard_map/slice | solution.py:63
  158.2 33.2 %collective-permute-start.11 = (f32[32,6,2,512]{3,0,2,1:T(8,128)S(1)}, f32[32,6,2,512]{3,0,2,1:T(8,128)S(1)}, u32[]{:S(2)}, u32[]{:S(2)}) collective-permute-start(f32[32,6,2,512]{3,0,2,1:T(8,128)S(1)} %get-tuple-element.20), channel_id=1, source_target_pairs={{1,0},{2,1},{3,2},{4,3},{5,4},{6,5},{7,6},{8,7},{9,8},{10,9},{11,1... | collective-permute-start | bytes 2359304 | tf_op jit(solution)/shard_map/ppermute | solution.py:20
  193.2 13.7 %collective-permute-start.12 = (f32[32,2,8,512]{3,0,2,1:T(8,128)S(1)}, f32[32,2,8,512]{3,0,2,1:T(8,128)S(1)}, u32[]{:S(2)}, u32[]{:S(2)}) collective-permute-start(f32[32,2,8,512]{3,0,2,1:T(8,128)S(1)} %fusion.32), channel_id=1, source_target_pairs={{0,16},{16,32},{32,48},{48,64},{64,80},{80,96},{96,112},{112,128},... | collective-permute-start | bytes 3145736 | tf_op jit(solution)/shard_map/ppermute | solution.py:19
  195.1 33.7 %collective-permute-start.13 = (f32[32,2,8,512]{3,0,2,1:T(8,128)S(1)}, f32[32,2,8,512]{3,0,2,1:T(8,128)S(1)}, u32[]{:S(2)}, u32[]{:S(2)}) collective-permute-start(f32[32,2,8,512]{3,0,2,1:T(8,128)S(1)} %fusion.32), channel_id=1, source_target_pairs={{16,0},{32,16},{48,32},{64,48},{80,64},{96,80},{112,96},{128,112},... | collective-permute-start | bytes 3145736 | tf_op jit(solution)/shard_map/ppermute | solution.py:20
  197.7 37.5 %copy-start.4 = (s32[1,1,8192]{2,1,0:T(1,128)S(1)}, s32[1,1,8192]{2,1,0:T(1,128)}, u32[]{:S(2)}) copy-start(s32[1,1,8192]{2,1,0:T(1,128)} %param.7) | copy-start | bytes 98308
  206.8 23.4 %copy-start.1 = (f32[32,2,8,512]{3,0,2,1:T(8,128)}, f32[32,2,8,512]{3,0,2,1:T(8,128)S(1)}, u32[]{:S(2)}) copy-start(f32[32,2,8,512]{3,0,2,1:T(8,128)S(1)} %collective-permute-done.12) | copy-start | bytes 3145732
  228.8 1.5 copy-start.2
  230.3 11.8 %collective-permute-start.14 = (f32[32,6,2,512]{3,0,2,1:T(8,128)}, f32[32,6,2,512]{3,0,2,1:T(8,128)}, u32[]{:S(2)}, u32[]{:S(2)}) collective-permute-start(f32[32,6,2,512]{3,0,2,1:T(8,128)} %get-tuple-element.17), channel_id=1, source_target_pairs={{0,1},{1,2},{2,3},{3,4},{4,5},{5,6},{6,7},{7,8},{8,9},{9,10},{10,1... | collective-permute-start | bytes 2359304 | tf_op jit(solution)/shard_map/ppermute | solution.py:19
  233.7 36.1 %collective-permute-start.15 = (f32[32,6,2,512]{3,0,2,1:T(8,128)}, f32[32,6,2,512]{3,0,2,1:T(8,128)}, u32[]{:S(2)}, u32[]{:S(2)}) collective-permute-start(f32[32,6,2,512]{3,0,2,1:T(8,128)} %get-tuple-element.18), channel_id=1, source_target_pairs={{1,0},{2,1},{3,2},{4,3},{5,4},{6,5},{7,6},{8,7},{9,8},{10,9},{11,1... | collective-permute-start | bytes 2359304 | tf_op jit(solution)/shard_map/ppermute | solution.py:20
  299.6 668.4 %all-reduce.9.cloned.1.call-start = ((), (), s32[]{:S(2)}) async-start(), calls=%async_computation.1 | async-start | bytes 2097152 | tf_op jit(solution)/shard_map/psum | solution.py:69
Sparse Core Ops, SparseCore 0:
  299.7 499.1 all-reduce.6
  802.1 165.8 all-reduce.8
